TPU v7x, 32 devices: a whole 2x2x4 slice. The times are simulated.
32 devices in a mesh: az: 8 (over z, y), ax: 4 (over x, core).
Axes of the slice: x: 2, y: 2, z: 4, core: 2. Of those that a mesh axis runs over, the one named last changes fastest.
Arguments:
- acoustic: float32 [4, 64, 64, 128], P(None, 'az', 'ax'), may hold values from -6 to 6
- mean_flow: float32 [4, 64, 64, 128], P(None, 'az', 'ax'), may hold values from -0.4 to 2, as said below
- adjoint_in: float32 [4, 64, 64, 128], P(None, 'az', 'ax'), may hold values from -6 to 6
- admittance: float32 [64], replicated, may hold values from 0.2 to 2
- segment_id: int32 [64, 64], P('az', 'ax'), may hold values from 0 to 63, as said below
- noise_code: int32 [64, 64], P('az', 'ax'), may hold values from 0 to 63
- noise_table: float32 [64], replicated, may hold values from -4 to 4
- mic_az: int32 [512], replicated, may hold values from 0 to 63, as said below
- mic_ax: int32 [512], replicated, may hold values from 0 to 63
- measured: float32 [512], replicated, may hold values from -17 to 17
Outputs:
- adjoint_out: float32 [4, 64, 64, 128], P(None, 'az', 'ax')
- liner_grad: float32 [64], replicated
- misfit: float32 [], replicated
Inputs may be any that keep to these rules, and one draw needn't show every extreme that they name: `mean_flow`: component 0 lies in 0.2 to 0.6, component 1 in -0.4 to 0.4, component 2 in 0.5 to 2, component 3 in 0.7 to 1.4. segment_id = sector * 4 + band, where the 16 sectors are runs of contiguous azimuthal cells (wrapping) and the 4 bands runs of contiguous axial cells; every segment has cells. `mic_az`: microphones sit on casing cells; several may share a cell.
All inputs are finite; a program needn't handle non-finite values.
Results may differ from a plain program's by a relative error of at most 0.000086.
Values sent between devices are 32-bit elements; how exact they have to be, the bound alone decides.
No kernel may reach another device: no remote copies, remote signals or barrier semaphores. Data moves between devices by JAX's collectives and lax.ppermute only.
A program may use at most 128 MiB of HBM per device.

v0:
```python
import jax
import jax.numpy as jnp
from jax import lax
from jax.sharding import PartitionSpec as P

step_dt = 0.25
epsilon = 1e-06
highest = lax.Precision.HIGHEST


def with_halo(array, sides, width, wrap):
    for axis, dim in sides:
        size, length = (lax.axis_size(axis), array.shape[dim])
        up = [(i, (i + 1) % size) for i in range(size if wrap else size - 1)]
        down = [(j, i) for i, j in up]
        last = lax.slice_in_dim(array, length - width, length, axis=dim)
        initial = lax.slice_in_dim(array, 0, width, axis=dim)
        before = lax.ppermute(last, axis, up)
        after = lax.ppermute(initial, axis, down)
        array = jnp.concatenate([before, array, after], axis=dim)
    return array


def center(values):
    return values[..., 1:-1, 1:-1, :]


def az_next(values):
    return values[..., 2:, 1:-1, :]


def az_prev(values):
    return values[..., :-2, 1:-1, :]


def ax_next(values):
    return values[..., 1:-1, 2:, :]


def ax_prev(values):
    return values[..., 1:-1, :-2, :]


def shrink(values, margin):
    return values[..., margin : values.shape[-3] - margin, margin : values.shape[-2] - margin, :]


def rad_next(values):
    return jnp.concatenate([values[..., 1:], jnp.zeros_like(values[..., :1])], axis=-1)


def rad_prev(values):
    return jnp.concatenate([jnp.zeros_like(values[..., :1]), values[..., :-1]], axis=-1)


def casing_mask(values):
    return lax.broadcasted_iota(jnp.int32, values.shape, values.ndim - 1) == values.shape[-1] - 1


def advect(values, axial_flow, swirl_flow):
    return (
        center(axial_flow) * (ax_next(values) - ax_prev(values)) * 0.5
        + center(swirl_flow) * (az_next(values) - az_prev(values)) * 0.5
    )


def advect_back(values, axial_flow, swirl_flow):
    carried_ax = axial_flow * values
    carried_az = swirl_flow * values
    return 0.5 * (ax_prev(carried_ax) - ax_next(carried_ax)) + 0.5 * (
        az_prev(carried_az) - az_next(carried_az)
    )


def exchange_rims(fields, rim_width):
    widened = with_halo(fields, (("ax", 2),), rim_width, False)
    return with_halo(widened, (("az", 1),), rim_width, True)


def forward_pressure(padded, wall_admit, source):
    pressure, vel_az, vel_ax, vel_rad = (padded[0], padded[1], padded[2], padded[3])
    axial_flow, swirl_flow, buoyancy, stiffness = (padded[4], padded[5], padded[6], padded[7])
    new_az = center(vel_az) - step_dt * (
        advect(vel_az, axial_flow, swirl_flow)
        + center(buoyancy) * (az_next(pressure) - center(pressure))
    )
    new_ax = center(vel_ax) - step_dt * (
        advect(vel_ax, axial_flow, swirl_flow)
        + center(buoyancy) * (ax_next(pressure) - center(pressure))
    )
    press_in = shrink(pressure, 1)
    rad_in = shrink(vel_rad, 1)
    axial_in = shrink(axial_flow, 1)
    swirl_in = shrink(swirl_flow, 1)
    buoy_in = shrink(buoyancy, 1)
    stiff_in = shrink(stiffness, 1)
    press_own = center(press_in)
    new_rad = jnp.where(
        casing_mask(press_own),
        wall_admit[:, :, None] * press_own,
        center(rad_in)
        - step_dt
        * (
            advect(rad_in, axial_in, swirl_in) + center(buoy_in) * (rad_next(press_own) - press_own)
        ),
    )
    spread = (
        center(new_az)
        - az_prev(new_az)
        + (center(new_ax) - ax_prev(new_ax))
        + (new_rad - rad_prev(new_rad))
    )
    return (
        press_own
        - step_dt * (advect(press_in, axial_in, swirl_in) + center(stiff_in) * spread)
        + step_dt * source
    )


def first_half(press_pad, vel_pad, coef_pad):
    pushed = step_dt * coef_pad[3] * press_pad
    pushed_own = center(pushed)
    head_az = vel_pad[0] - (pushed_own - az_next(pushed))
    head_ax = vel_pad[1] - (pushed_own - ax_next(pushed))
    head_rad = vel_pad[2] - (pushed_own - rad_next(pushed_own))
    return jnp.stack([head_az, head_ax, head_rad])


def second_half(press_pad, head_stack, coef_pad, wall_admit):
    axial_flow, swirl_flow, buoyancy = (coef_pad[0], coef_pad[1], coef_pad[2])
    head_az, head_ax = (head_stack[0], head_stack[1])
    head_masked = jnp.where(casing_mask(head_stack[2]), 0.0, head_stack[2])
    back_az = center(head_az) - step_dt * advect_back(head_az, axial_flow, swirl_flow)
    back_ax = center(head_ax) - step_dt * advect_back(head_ax, axial_flow, swirl_flow)
    back_rad = center(head_masked) - step_dt * advect_back(head_masked, axial_flow, swirl_flow)
    push_az = step_dt * buoyancy * head_az
    push_ax = step_dt * buoyancy * head_ax
    push_rad = step_dt * center(buoyancy) * center(head_masked)
    rad_own = center(head_stack[2])
    back_press = center(press_pad) - step_dt * advect_back(press_pad, axial_flow, swirl_flow)
    back_press = (
        back_press
        + (center(push_az) - az_prev(push_az))
        + (center(push_ax) - ax_prev(push_ax))
        + (push_rad - rad_prev(push_rad))
    )
    back_press = back_press + jnp.where(casing_mask(rad_own), wall_admit[:, :, None] * rad_own, 0.0)
    return (jnp.stack([back_press, back_az, back_ax, back_rad]), rad_own[..., -1])


def adjoint_step(seed_list, velocity_list, coef_wide, wall_admit, rim_width):
    joined = exchange_rims(jnp.stack(seed_list), rim_width)
    coef_first = shrink(coef_wide, 2 - rim_width)
    coef_second = shrink(coef_wide, 1)
    member = 0
    head_list = first_half(joined[member], velocity_list[member], coef_first)
    widened = exchange_rims(head_list, 1)
    member = 0
    results = [second_half(joined[member], widened, coef_second, wall_admit)]
    return results


def shards(
    acoustic,
    mean_flow,
    adjoint_in,
    admittance,
    segment_id,
    noise_code,
    noise_table,
    mic_az,
    mic_ax,
    measured,
):
    az_cells, ax_cells, rad_cells = (acoustic.shape[1], acoustic.shape[2], acoustic.shape[3])
    buoyancy = 1.0 / mean_flow[2]
    stiffness = mean_flow[2] * mean_flow[3] * mean_flow[3]
    segment_hot = (
        segment_id[:, :, None] == lax.broadcasted_iota(jnp.int32, (1, 1, admittance.shape[0]), 2)
    ).astype(jnp.float32)
    wall_admit = jnp.dot(segment_hot, admittance, precision=highest)
    noise_hot = (
        noise_code[:, :, None] == lax.broadcasted_iota(jnp.int32, (1, 1, noise_table.shape[0]), 2)
    ).astype(jnp.float32)
    profile = (lax.broadcasted_iota(jnp.float32, (rad_cells,), 0) + 0.5) / rad_cells
    source = jnp.dot(noise_hot, noise_table, precision=highest)[:, :, None] * profile
    coefficients = jnp.stack([mean_flow[0], mean_flow[1], buoyancy, stiffness])
    rim_width = 1
    padded = exchange_rims(jnp.concatenate([acoustic, coefficients], axis=0), 2)
    velocities = adjoint_in[1:]
    coef_wide = padded[4:8]
    new_press = forward_pressure(padded, wall_admit, source)
    first_az = lax.axis_index("az") * az_cells
    first_ax = lax.axis_index("ax") * ax_cells
    local_az = mic_az - first_az
    local_ax = mic_ax - first_ax
    owned = (local_az >= 0) & (local_az < az_cells) & (local_ax >= 0) & (local_ax < ax_cells)
    flat_cell = jnp.clip(local_az, 0, az_cells - 1) * ax_cells + jnp.clip(local_ax, 0, ax_cells - 1)
    heard = new_press[:, :, rad_cells - 1].reshape(az_cells * ax_cells)[flat_cell]
    misses = jnp.where(owned, heard - measured, 0.0)
    square_sum = jnp.sum(misses * misses)
    mic_count = mic_az.shape[0]
    casing_own = acoustic[0][:, :, rad_cells - 1]
    grad_scale = (
        az_cells * lax.axis_size("az") * ax_cells * lax.axis_size("ax") / admittance.shape[0]
    ) ** (-0.5)
    total_sq = lax.psum(square_sum, ("az", "ax"))
    mean_sq = total_sq / mic_count + epsilon
    placed = (
        jnp.zeros((az_cells * ax_cells,), jnp.float32)
        .at[flat_cell]
        .add(jnp.where(owned, misses / mean_sq, 0.0))
        .reshape(az_cells, ax_cells)
    )
    seed_press = adjoint_in[0] + jnp.where(casing_mask(adjoint_in[0]), placed[:, :, None], 0.0)
    outcome = adjoint_step([seed_press], [velocities], coef_wide, wall_admit, rim_width)
    adjoint_out, rad_top = outcome[0]
    segment_sums = jnp.einsum("acs,ac->s", segment_hot, rad_top * casing_own, precision=highest)
    liner_grad = lax.psum(segment_sums, ("az", "ax")) * grad_scale
    misfit = 0.5 * jnp.log(mean_sq)
    return (adjoint_out, liner_grad, misfit)


def solution(mesh):
    placed = (
        P(None, "az", "ax", None),
        P(None, "az", "ax", None),
        P(None, "az", "ax", None),
        P(),
        P("az", "ax"),
        P("az", "ax"),
        P(),
        P(),
        P(),
        P(),
    )
    return jax.shard_map(
        shards,
        mesh=mesh,
        in_specs=placed,
        out_specs=(P(None, "az", "ax", None), P(), P()),
        check_vma=False,
    )
```

profile of v0, /device:TPU:14, one launch (start us, length us, event | category | flops | bytes accessed | tf_op | source)
XLA Modules:
  0.0 222.4 jit_solution(4559688916384890473)
XLA Ops:
  0.6 0.9 slice_divide_fusion
  1.5 0.9 slice.363
  2.5 1.0 pad_maximum_fusion.6
  3.7 1.9 collective-permute-start.1
  5.6 2.4 %collective-permute-start = (f32[8,8,2,128]{3,1,2,0:T(8,128)S(1)}, f32[8,8,2,128]{3,1,2,0:T(8,128)S(1)}, u32[]{:S(2)}, u32[]{:S(2)}) collective-permute-start(f32[8,8,2,128]{3,1,2,0:T(8,128)S(1)} %copy.107), channel_id=1, source_target_pairs={{0,1},{1,2},{2,3},{4,5},{5,6},{6,7},{8,9},{9,10},{10,11},{12,13},{... | collective-permute-start | bytes 196616 | tf_op jit(solution)/shard_map/ppermute | solution.py:18
  8.0 2.7 %copy.81 = f32[8,8,16,128]{2,1,3,0:T(8,128)} copy(f32[8,8,16,128]{3,2,1,0:T(8,128)S(1)} %pad_maximum_fusion.6) | data formatting | bytes 1048576 | tf_op jit(solution)/shard_map/concatenate | solution.py:189
  11.1 0.4 fusion.65
  11.6 2.7 %copy.82 = f32[8,8,2,128]{2,1,3,0:T(8,128)} copy(f32[8,8,2,128]{3,1,2,0:T(8,128)S(1)} %collective-permute-done.1) | data formatting | bytes 131072 | tf_op jit(solution)/shard_map/ppermute | solution.py:19
  14.3 2.7 %copy.80 = f32[8,8,2,128]{2,1,3,0:T(8,128)} copy(f32[8,8,2,128]{3,1,2,0:T(8,128)S(1)} %collective-permute-done) | data formatting | bytes 131072 | tf_op jit(solution)/shard_map/ppermute | solution.py:18
  17.0 12.7 %pad_maximum_fusion.5 = (f32[8,2,20,128]{2,1,3,0:T(2,128)S(1)}, f32[8,2,20,128]{2,1,3,0:T(2,128)S(1)}) fusion(f32[8,8,2,128]{2,1,3,0:T(8,128)} %copy.82, f32[8,8,16,128]{2,1,3,0:T(8,128)} %copy.81, f32[8,8,2,128]{2,1,3,0:T(8,128)} %copy.80), kind=kLoop, calls=%fused_computation.47 | loop fusion | flops 163840 | bytes 983040 | tf_op jit(solution)/shard_map/slice | solution.py:16
  30.1 0.6 collective-permute-start.3
  31.0 2.6 %collective-permute-start.2 = (f32[8,2,20,128]{3,0,2,1:T(8,128)S(1)}, f32[8,2,20,128]{3,0,2,1:T(8,128)S(1)}, u32[]{:S(2)}, u32[]{:S(2)}) collective-permute-start(f32[8,2,20,128]{3,0,2,1:T(8,128)S(1)} %copy.83), channel_id=1, source_target_pairs={{0,4},{4,8},{8,12},{12,16},{16,20},{20,24},{24,28},{28,0},{1,5},{5... | collective-permute-start | bytes 491528 | tf_op jit(solution)/shard_map/ppermute | solution.py:18
  33.7 0.6 slice.520
  34.2 2.9 %collective-permute-done.3 = f32[8,2,20,128]{3,0,2,1:T(8,128)S(1)} collective-permute-done((f32[8,2,20,128]{3,0,2,1:T(8,128)S(1)}, f32[8,2,20,128]{3,0,2,1:T(8,128)S(1)}, u32[]{:S(2)}, u32[]{:S(2)}) %collective-permute-start.3) | collective-permute-done | bytes 163872 | tf_op jit(solution)/shard_map/ppermute | solution.py:19
  37.1 0.5 copy.86
  37.6 2.3 %collective-permute-done.2 = f32[8,2,20,128]{3,0,2,1:T(8,128)S(1)} collective-permute-done((f32[8,2,20,128]{3,0,2,1:T(8,128)S(1)}, f32[8,2,20,128]{3,0,2,1:T(8,128)S(1)}, u32[]{:S(2)}, u32[]{:S(2)}) %collective-permute-start.2) | collective-permute-done | bytes 163872 | tf_op jit(solution)/shard_map/ppermute | solution.py:18
  39.9 0.5 copy.85
  40.4 7.7 %pad_maximum_fusion = f32[8,12,20,128]{2,1,3,0:T(8,128)S(1)} fusion(f32[8,2,20,128]{2,1,3,0:T(2,128)S(1)} %copy.86, f32[8,8,2,128]{2,1,3,0:T(8,128)} %copy.82, f32[8,8,16,128]{2,1,3,0:T(8,128)} %copy.81, f32[8,8,2,128]{2,1,3,0:T(8,128)} %copy.80, f32[8,2,20,128]{2,1,3,0:T(2,128)S(1)} %copy.85), kind=kLoop, calls=%fused_computation.2 | loop fusion | flops 983040 | bytes 1966080 | tf_op jit(solution)/shard_map/concatenate | solution.py:20
  48.1 0.6 slice_bitcast_fusion.9
  48.7 2.7 %copy-done.2 = f32[8,12,20,128]{2,1,3,0:T(8,128)} copy-done((f32[8,12,20,128]{2,1,3,0:T(8,128)}, f32[8,12,20,128]{2,1,3,0:T(8,128)S(1)}, u32[]{:S(2)}) %copy-start.2) | copy-done | bytes 983064
  51.8 2.5 %fusion.5 = f32[10,18,128]{1,0,2:T(8,128)S(1)} fusion(f32[12,20,128]{1,0,2:T(8,128)S(1)} %get-tuple-element.33, f32[12,20,128]{1,0,2:T(8,128)S(1)} %get-tuple-element.28, f32[12,20,128]{1,0,2:T(8,128)S(1)} %get-tuple-element.29, f32[12,20,128]{1,0,2:T(8,128)S(1)} %get-tuple-element.31, f32[12,20,128]{1,0,2:T(8,128)S(1)} %get-tuple-element.32), kind=kLoop, calls=%fused_computation.20 | loop fusion | flops 253440 | bytes 1013760 | tf_op jit(solution)/shard_map/sub | solution.py:87
  54.3 2.5 %fusion.13 = f32[10,18,128]{1,0,2:T(8,128)S(1)} fusion(f32[12,20,128]{1,0,2:T(8,128)S(1)} %get-tuple-element.33, f32[12,20,128]{1,0,2:T(8,128)S(1)} %get-tuple-element.26, f32[12,20,128]{1,0,2:T(8,128)S(1)} %get-tuple-element.29, f32[12,20,128]{1,0,2:T(8,128)S(1)} %get-tuple-element.31, f32[12,20,128]{1,0,2:T(8,128)S(1)} %get-tuple-element.32), kind=kLoop, calls=%fused_computation.32 | loop fusion | flops 253440 | bytes 1013760 | tf_op jit(solution)/shard_map/sub | solution.py:83
  56.8 2.0 fusion.62
  58.8 0.5 fusion.60
  59.3 0.7 fusion.69
  60.0 3.3 %gather_fusion = f32[512]{0:T(512)S(1)} fusion(f32[128]{0:T(128)S(1)} %reshape_squeeze.3, s32[1024]{0:T(1024)S(1)} %pad_clamp_fusion), kind=kCustom, calls=%fused_computation | custom fusion | bytes 6144 | tf_op jit(solution)/shard_map/gather | solution.py:199
  63.4 0.6 multiply_reduce_fusion
  64.0 43.0 %psum.14 = f32[]{:T(128)} all-reduce(f32[]{:T(128)} %get-tuple-element.11), channel_id=1, replica_groups=mesh['az'=8,'ax'=4] {'az','ax'}, use_global_device_ids=true, to_apply=%region_1.2 | all-reduce | flops 1 | bytes 8 | tf_op jit(solution)/shard_map/psum | solution.py:207
  107.7 4.1 %scatter_custom_fusion = f32[128]{0:T(128)S(1)} fusion(s32[512]{0:T(512)S(1)} %compare_select_fusion, f32[512]{0:T(512)S(1)} %divide_select_fusion, f32[]{:T(128)} %constant.19.clone.1), kind=kCustom, calls=%fused_computation.159 | custom fusion | flops 512 | bytes 516 | tf_op jit(solution)/shard_map/scatter-add | solution.py:212
  112.1 1.9 collective-permute-start.5
  114.0 2.4 %collective-permute-start.4 = (f32[1,8,1,128]{3,1,2,0:T(8,128)S(1)}, f32[1,8,1,128]{3,1,2,0:T(8,128)S(1)}, u32[]{:S(2)}, u32[]{:S(2)}) collective-permute-start(f32[1,8,1,128]{3,1,2,0:T(8,128)S(1)} %get-tuple-element.60), channel_id=1, source_target_pairs={{0,1},{1,2},{2,3},{4,5},{5,6},{6,7},{8,9},{9,10},{10,11},{12,13},{... | collective-permute-start | bytes 12296 | tf_op jit(solution)/shard_map/ppermute | solution.py:18
  116.4 2.9 %collective-permute-done.4 = f32[1,8,1,128]{3,1,2,0:T(8,128)S(1)} collective-permute-done((f32[1,8,1,128]{3,1,2,0:T(8,128)S(1)}, f32[1,8,1,128]{3,1,2,0:T(8,128)S(1)}, u32[]{:S(2)}, u32[]{:S(2)}) %collective-permute-start.4) | collective-permute-done | bytes 4128 | tf_op jit(solution)/shard_map/ppermute | solution.py:18
  119.4 1.5 collective-permute-start.7
  121.0 1.5 collective-permute-start.6
  123.3 1.0 copy.112
  124.6 0.7 collective-permute-done.6
  125.3 4.2 %fusion.21 = (f32[10,18,128]{1,0,2:T(8,128)}, f32[10,18,128]{1,0,2:T(8,128)S(1)}, f32[10,18,128]{1,0,2:T(8,128)}) fusion(f32[8,12,20,128]{2,1,3,0:T(8,128)} %copy-done.2, f32[1,1,18,128]{2,1,3,0:T(1,128)S(1)} %collective-permute-done.7, f32[1,8,18,128]{2,1,3,0:T(8,128)S(1)} %copy.90, f32[1,1,18,128]{2,1,3,0:T(1,128)S(1)} %collective-permute-done.6), kind=kLoop, calls=%fused_computation.54 | loop fusion | flops 138240 | bytes 645120 | tf_op jit(solution)/shard_map/mul | solution.py:68
  129.7 0.5 fusion.48
  130.3 0.5 fusion.77
  131.3 0.5 copy.95
  131.8 2.1 collective-permute-start.9
  134.0 0.5 copy.94
  134.5 2.2 collective-permute-start.8
  136.7 2.6 %slice_bitcast_fusion.3 = f32[10,18,128]{1,0,2:T(8,128)} fusion(f32[8,12,20,128]{2,1,3,0:T(8,128)} %copy-done.2), kind=kLoop, calls=%fused_computation.12 | loop fusion | bytes 184320 | tf_op jit(solution)/shard_map/squeeze | solution.py:130
  139.3 0.6 copy.97
  139.9 0.6 copy.96
  140.5 3.8 %pad_maximum_fusion.12 = (f32[3,1,18,128]{2,1,3,0:T(1,128)S(1)}, f32[3,1,18,128]{2,1,3,0:T(1,128)S(1)}) fusion(f32[3,8,1,128]{2,1,3,0:T(8,128)S(1)} %copy.97, f32[3,8,1,128]{2,1,3,0:T(8,128)S(1)} %copy.96, f32[1,8,16,128]{2,1,3,0:T(8,128)} %copy-done.7, f32[1,8,16,128]{2,1,3,0:T(8,128)} %copy-done.5, f32[1,8,16,128]{2,1,3,0:T(8,128)} %copy-done.3), kind=kLoop, calls=%fused_computation.127 | loop fusion | flops 55296 | bytes 276480 | tf_op jit(solution)/shard_map/slice | solution.py:16
  144.3 1.0 collective-permute-start.11
  145.3 2.0 collective-permute-start.10
  147.3 1.2 maximum_bitcast_fusion
  148.5 4.7 %collective-permute-done.11 = f32[3,1,18,128]{2,1,3,0:T(1,128)S(1)} collective-permute-done((f32[3,1,18,128]{2,1,3,0:T(1,128)S(1)}, f32[3,1,18,128]{2,1,3,0:T(1,128)S(1)}, u32[]{:S(2)}, u32[]{:S(2)}) %collective-permute-start.11) | collective-permute-done | bytes 27680 | tf_op jit(solution)/shard_map/ppermute | solution.py:19
  153.2 2.2 collective-permute-done.10
  155.4 1.7 pad_maximum_fusion.1
  157.2 4.9 %multiply_multiply_fusion.1 = (f32[10,18,128]{1,0,2:T(8,128)}, f32[10,18,128]{1,0,2:T(8,128)}, f32[10,18,128]{1,0,2:T(8,128)S(1)}, f32[10,18,128]{1,0,2:T(8,128)...) fusion(f32[8,12,20,128]{2,1,3,0:T(8,128)} %copy-done.2, ...), kind=kLoop, calls=%fused_computation.50 | loop fusion | flops 207360 | bytes 1290368 | tf_op jit(solution)/shard_map/mul | solution.py:136
  162.1 1.8 slice_bitcast_fusion
  163.9 1.7 fusion.22
  165.6 0.7 fusion.41
  166.5 3.1 %fusion.33 = f32[1,8,16,128]{2,1,3,0:T(8,128)S(1)} fusion(f32[10,18,128]{1,0,2:T(8,128)} %get-tuple-element.18, f32[10,18,128]{1,0,2:T(8,128)} %get-tuple-element.20, f32[10,18,128]{1,0,2:T(8,128)} %get-tuple-element.37), kind=kLoop, calls=%fused_computation.69 | loop fusion | flops 81920 | bytes 393216 | tf_op jit(solution)/shard_map/stack | solution.py:148
  169.7 1.9 fusion.37
  171.9 5.0 %fusion.40 = f32[1,8,16,128]{2,1,3,0:T(8,128)S(1)} fusion(f32[10,18,128]{1,0,2:T(8,128)} %get-tuple-element.36, f32[10,18,128]{1,0,2:T(8,128)} %get-tuple-element.16, f32[10,18,128]{1,0,2:T(8,128)} %get-tuple-element.15, f32[10,18,128]{1,0,2:T(8,128)} %get-tuple-element.25, f32[10,18,128]{1,0,2:T(8,128)} %get-tuple-element.23, ...), kind=kLoop, calls=%fused_computation.80 | loop fusion | flops 229376 | bytes 852096 | tf_op jit(solution)/shard_map/stack | solution.py:148
  177.1 0.8 slice_multiply_fusion.4
  178.1 41.9 %psum.15 = f32[64]{0:T(128)S(1)} all-reduce(f32[64]{0:T(128)S(1)} %convolution_bitcast_fusion), channel_id=1, replica_groups=mesh['az'=8,'ax'=4] {'az','ax'}, use_global_device_ids=true, to_apply=%region_3.4 | all-reduce | flops 64 | bytes 512 | tf_op jit(solution)/shard_map/psum | solution.py:219
  220.0 0.5 broadcast_multiply_fusion
  220.5 0.7 pad_maximum_fusion.7
  (81 shorter events, 5.2 us)
Async XLA Ops:
  0.6 10.1 %copy-start = (f32[64]{0:T(128)S(1)}, f32[64]{0:T(128)}, u32[]{:S(2)}) copy-start(f32[64]{0:T(128)} %param.13) | copy-start | bytes 772
  2.5 8.2 %copy-start.12 = (f32[4,8,16,128]{3,2,1,0:T(8,128)S(1)}, f32[4,8,16,128]{3,2,1,0:T(8,128)}, u32[]{:S(2)}) copy-start(f32[4,8,16,128]{3,2,1,0:T(8,128)} %param.12) | copy-start | bytes 786436
  3.5 7.2 %copy-start.17 = (s32[8,16]{1,0:T(8,128)S(1)}, s32[8,16]{1,0:T(8,128)}, u32[]{:S(2)}) copy-start(s32[8,16]{1,0:T(8,128)} %param.14) | copy-start | bytes 1540
  3.5 7.6 %copy-start.16 = (s32[8,16]{1,0:T(8,128)S(1)}, s32[8,16]{1,0:T(8,128)}, u32[]{:S(2)}) copy-start(s32[8,16]{1,0:T(8,128)} %param.15) | copy-start | bytes 1540
  3.5 7.6 %copy-start.18 = (f32[64]{0:T(128)S(1)}, f32[64]{0:T(128)}, u32[]{:S(2)}) copy-start(f32[64]{0:T(128)} %param.16) | copy-start | bytes 772
  3.6 8.0 %copy-start.13 = (s32[512]{0:T(512)S(1)}, s32[512]{0:T(512)}, u32[]{:S(2)}) copy-start(s32[512]{0:T(512)} %param.18) | copy-start | bytes 6148
  3.6 8.0 %copy-start.14 = (s32[512]{0:T(512)S(1)}, s32[512]{0:T(512)}, u32[]{:S(2)}) copy-start(s32[512]{0:T(512)} %param.17) | copy-start | bytes 6148
  3.7 8.0 %collective-permute-start.1 = (f32[8,8,2,128]{3,1,2,0:T(8,128)S(1)}, f32[8,8,2,128]{3,1,2,0:T(8,128)S(1)}, u32[]{:S(2)}, u32[]{:S(2)}) collective-permute-start(f32[8,8,2,128]{3,1,2,0:T(8,128)S(1)} %copy.108), channel_id=1, source_target_pairs={{1,0},{2,1},{3,2},{5,4},{6,5},{7,6},{9,8},{10,9},{11,10},{13,12},{... | collective-permute-start | bytes 196616 | tf_op jit(solution)/shard_map/ppermute | solution.py:19
  5.6 8.7 %collective-permute-start = (f32[8,8,2,128]{3,1,2,0:T(8,128)S(1)}, f32[8,8,2,128]{3,1,2,0:T(8,128)S(1)}, u32[]{:S(2)}, u32[]{:S(2)}) collective-permute-start(f32[8,8,2,128]{3,1,2,0:T(8,128)S(1)} %copy.107), channel_id=1, source_target_pairs={{0,1},{1,2},{2,3},{4,5},{5,6},{6,7},{8,9},{9,10},{10,11},{12,13},{... | collective-permute-start | bytes 196616 | tf_op jit(solution)/shard_map/ppermute | solution.py:18
  30.1 7.1 %collective-permute-start.3 = (f32[8,2,20,128]{3,0,2,1:T(8,128)S(1)}, f32[8,2,20,128]{3,0,2,1:T(8,128)S(1)}, u32[]{:S(2)}, u32[]{:S(2)}) collective-permute-start(f32[8,2,20,128]{3,0,2,1:T(8,128)S(1)} %copy.84), channel_id=1, source_target_pairs={{4,0},{8,4},{12,8},{16,12},{20,16},{24,20},{28,24},{0,28},{5,1},{9... | collective-permute-start | bytes 491528 | tf_op jit(solution)/shard_map/ppermute | solution.py:19
  31.0 9.0 %collective-permute-start.2 = (f32[8,2,20,128]{3,0,2,1:T(8,128)S(1)}, f32[8,2,20,128]{3,0,2,1:T(8,128)S(1)}, u32[]{:S(2)}, u32[]{:S(2)}) collective-permute-start(f32[8,2,20,128]{3,0,2,1:T(8,128)S(1)} %copy.83), channel_id=1, source_target_pairs={{0,4},{4,8},{8,12},{12,16},{16,20},{20,24},{24,28},{28,0},{1,5},{5... | collective-permute-start | bytes 491528 | tf_op jit(solution)/shard_map/ppermute | solution.py:18
  48.1 3.3 %copy-start.2 = (f32[8,12,20,128]{2,1,3,0:T(8,128)}, f32[8,12,20,128]{2,1,3,0:T(8,128)S(1)}, u32[]{:S(2)}) copy-start(f32[8,12,20,128]{2,1,3,0:T(8,128)S(1)} %pad_maximum_fusion) | copy-start | bytes 2949124
  58.8 4.6 %copy-start.15 = (f32[512]{0:T(512)S(1)}, f32[512]{0:T(512)}, u32[]{:S(2)}) copy-start(f32[512]{0:T(512)} %param.19) | copy-start | bytes 6148
  59.3 64.0 %slice-start = ((f32[4,8,16,128]{3,2,1,0:T(8,128)}), f32[1,8,16,128]{3,2,1,0:T(8,128)S(1)}, s32[]{:S(2)}) async-start(f32[4,8,16,128]{3,2,1,0:T(8,128)} %param.10), calls=%async_computation | async-start | bytes 131072 | tf_op jit(solution)/shard_map/slice | solution.py:203
  112.1 4.3 %collective-permute-start.5 = (f32[1,8,1,128]{3,1,2,0:T(8,128)S(1)}, f32[1,8,1,128]{3,1,2,0:T(8,128)S(1)}, u32[]{:S(2)}, u32[]{:S(2)}) collective-permute-start(f32[1,8,1,128]{3,1,2,0:T(8,128)S(1)} %get-tuple-element.61), channel_id=1, source_target_pairs={{1,0},{2,1},{3,2},{5,4},{6,5},{7,6},{9,8},{10,9},{11,10},{13,12},{... | collective-permute-start | bytes 12296 | tf_op jit(solution)/shard_map/ppermute | solution.py:19
  114.0 5.3 %collective-permute-start.4 = (f32[1,8,1,128]{3,1,2,0:T(8,128)S(1)}, f32[1,8,1,128]{3,1,2,0:T(8,128)S(1)}, u32[]{:S(2)}, u32[]{:S(2)}) collective-permute-start(f32[1,8,1,128]{3,1,2,0:T(8,128)S(1)} %get-tuple-element.60), channel_id=1, source_target_pairs={{0,1},{1,2},{2,3},{4,5},{5,6},{6,7},{8,9},{9,10},{10,11},{12,13},{... | collective-permute-start | bytes 12296 | tf_op jit(solution)/shard_map/ppermute | solution.py:18
  119.4 5.2 %collective-permute-start.7 = (f32[1,1,18,128]{2,1,3,0:T(1,128)S(1)}, f32[1,1,18,128]{2,1,3,0:T(1,128)S(1)}, u32[]{:S(2)}, u32[]{:S(2)}) collective-permute-start(f32[1,1,18,128]{2,1,3,0:T(1,128)S(1)} %copy.89), channel_id=1, source_target_pairs={{4,0},{8,4},{12,8},{16,12},{20,16},{24,20},{28,24},{0,28},{5,1},{9... | collective-permute-start | bytes 27656 | tf_op jit(solution)/shard_map/ppermute | solution.py:19
  121.0 4.3 %collective-permute-start.6 = (f32[1,1,18,128]{2,1,3,0:T(1,128)S(1)}, f32[1,1,18,128]{2,1,3,0:T(1,128)S(1)}, u32[]{:S(2)}, u32[]{:S(2)}) collective-permute-start(f32[1,1,18,128]{2,1,3,0:T(1,128)S(1)} %copy.88), channel_id=1, source_target_pairs={{0,4},{4,8},{8,12},{12,16},{16,20},{20,24},{24,28},{28,0},{1,5},{5... | collective-permute-start | bytes 27656 | tf_op jit(solution)/shard_map/ppermute | solution.py:18
  124.5 5.0 %copy-start.9 = (f32[1,8,18,128]{2,1,3,0:T(8,128)}, f32[1,8,18,128]{2,1,3,0:T(8,128)S(1)}, u32[]{:S(2)}) copy-start(f32[1,8,18,128]{2,1,3,0:T(8,128)S(1)} %copy.90) | copy-start | bytes 221188
  130.2 0.8 copy-start.3
  130.2 1.0 copy-start.5
  130.2 1.1 copy-start.7
  131.8 7.5 %collective-permute-start.9 = (f32[3,8,1,128]{3,1,2,0:T(8,128)S(1)}, f32[3,8,1,128]{3,1,2,0:T(8,128)S(1)}, u32[]{:S(2)}, u32[]{:S(2)}) collective-permute-start(f32[3,8,1,128]{3,1,2,0:T(8,128)S(1)} %copy.95), channel_id=1, source_target_pairs={{1,0},{2,1},{3,2},{5,4},{6,5},{7,6},{9,8},{10,9},{11,10},{13,12},{... | collective-permute-start | bytes 36872 | tf_op jit(solution)/shard_map/ppermute | solution.py:19
  134.5 5.4 %collective-permute-start.8 = (f32[3,8,1,128]{3,1,2,0:T(8,128)S(1)}, f32[3,8,1,128]{3,1,2,0:T(8,128)S(1)}, u32[]{:S(2)}, u32[]{:S(2)}) collective-permute-start(f32[3,8,1,128]{3,1,2,0:T(8,128)S(1)} %copy.94), channel_id=1, source_target_pairs={{0,1},{1,2},{2,3},{4,5},{5,6},{6,7},{8,9},{9,10},{10,11},{12,13},{... | collective-permute-start | bytes 36872 | tf_op jit(solution)/shard_map/ppermute | solution.py:18
  140.5 6.8 %copy-start.10 = (f32[1,8,18,128]{2,1,3,0:T(8,128)S(1)}, f32[1,8,18,128]{2,1,3,0:T(8,128)}, u32[]{:S(2)}) copy-start(f32[1,8,18,128]{2,1,3,0:T(8,128)} %copy-done.9) | copy-start | bytes 221188
  140.5 14.9 %copy-start.4 = (f32[1,8,16,128]{2,1,3,0:T(8,128)S(1)}, f32[1,8,16,128]{2,1,3,0:T(8,128)}, u32[]{:S(2)}) copy-start(f32[1,8,16,128]{2,1,3,0:T(8,128)} %copy-done.3) | copy-start | bytes 196612
  140.5 14.9 %copy-start.6 = (f32[1,8,16,128]{2,1,3,0:T(8,128)S(1)}, f32[1,8,16,128]{2,1,3,0:T(8,128)}, u32[]{:S(2)}) copy-start(f32[1,8,16,128]{2,1,3,0:T(8,128)} %copy-done.5) | copy-start | bytes 196612
  140.5 14.9 %copy-start.8 = (f32[1,8,16,128]{2,1,3,0:T(8,128)S(1)}, f32[1,8,16,128]{2,1,3,0:T(8,128)}, u32[]{:S(2)}) copy-start(f32[1,8,16,128]{2,1,3,0:T(8,128)} %copy-done.7) | copy-start | bytes 196612
  144.3 8.9 %collective-permute-start.11 = (f32[3,1,18,128]{2,1,3,0:T(1,128)S(1)}, f32[3,1,18,128]{2,1,3,0:T(1,128)S(1)}, u32[]{:S(2)}, u32[]{:S(2)}) collective-permute-start(f32[3,1,18,128]{2,1,3,0:T(1,128)S(1)} %get-tuple-element.35), channel_id=1, source_target_pairs={{4,0},{8,4},{12,8},{16,12},{20,16},{24,20},{28,24},{0,28},{5,1},{9... | collective-permute-start | bytes 82952 | tf_op jit(solution)/shard_map/ppermute | solution.py:19
  145.3 10.1 %collective-permute-start.10 = (f32[3,1,18,128]{2,1,3,0:T(1,128)S(1)}, f32[3,1,18,128]{2,1,3,0:T(1,128)S(1)}, u32[]{:S(2)}, u32[]{:S(2)}) collective-permute-start(f32[3,1,18,128]{2,1,3,0:T(1,128)S(1)} %get-tuple-element.34), channel_id=1, source_target_pairs={{0,4},{4,8},{8,12},{12,16},{16,20},{20,24},{24,28},{28,0},{1,5},{5... | collective-permute-start | bytes 82952 | tf_op jit(solution)/shard_map/ppermute | solution.py:18
  163.9 1.7 copy-start.11
  171.9 49.4 %copy-start.1 = (f32[64]{0:T(128)S(1)}, f32[64]{0:T(128)}, u32[]{:S(2)}) copy-start(f32[64]{0:T(128)} %param.13) | copy-start | bytes 772
where the time goes:
time: 223 us; the launch traced here: 222 us
  blocking collectives  85 us (38%)
  other arithmetic  66.1 us (30%)
  local copies, waits for them, and re-layouts  29.3 us (13%)
  starting transfers between devices  22.2 us (10%)
  waiting for transfers between devices  15.7 us (7%)
  between operations  3.04 us (1%)
    psum x1, blocking collectives, shards(): total_sq = lax.psum(square_sum, ('az', 'ax'))  43 us
    psum x1, blocking collectives, shards(): liner_grad = lax.psum(segment_sums, ('az', 'ax')) * grad_scale  41.9 us
    slice x2, other arithmetic, with_halo(): last = lax.slice_in_dim(array, length - width, length, axis=dim)  16.5 us
    ppermute x6, starting transfers between devices, with_halo(): before = lax.ppermute(last, axis, up)  13.2 us
    another operation x4, other arithmetic, second_half(): jnp.stack([back_press, back_az, back_ax, back_rad])  10.7 us
    concatenate x3, other arithmetic, with_halo(): array = jnp.concatenate([before, array, after], axis=dim)  9.38 us
    ppermute x6, starting transfers between devices, with_halo(): after = lax.ppermute(initial, axis, down)  8.97 us
    ppermute x6, waiting for transfers between devices, with_halo(): before = lax.ppermute(last, axis, up)  8.08 us
  transfers between devices with their start and end apart: 12, of which 7 were waited for; matrix products, arithmetic and copies ran while one was open for 7% of the time, Pallas kernels for 0%

commit v1 on v0

--- a/solution.py
+++ b/solution.py
@@ -6,6 +6,12 @@
 step_dt = 0.25
 epsilon = 1e-06
 highest = lax.Precision.HIGHEST
+
+
+def define_the_loads(local_array):
+    for j0 in ("ax", "az"):
+        local_array = lax.psum(local_array, axis_name=j0)
+    return local_array
 
 
 def with_halo(array, sides, width, wrap):
@@ -216,7 +222,7 @@
     outcome = adjoint_step([seed_press], [velocities], coef_wide, wall_admit, rim_width)
     adjoint_out, rad_top = outcome[0]
     segment_sums = jnp.einsum("acs,ac->s", segment_hot, rad_top * casing_own, precision=highest)
-    liner_grad = lax.psum(segment_sums, ("az", "ax")) * grad_scale
+    liner_grad = define_the_loads(segment_sums) * grad_scale
     misfit = 0.5 * jnp.log(mean_sq)
     return (adjoint_out, liner_grad, misfit)
 

time: 223 us -> 211 us (0.946)
  the two profiles are of different devices: /device:TPU:14 before, /device:TPU:0 now
where the time goes in v1:
time: 211 us; the launch traced here: 210 us
  other arithmetic  66.1 us (31%)
  blocking collectives  64 us (30%)
  local copies, waits for them, and re-layouts  29.3 us (14%)
  starting transfers between devices  25.7 us (12%)
  waiting for transfers between devices  20.7 us (10%)
  between operations  3.07 us (1%)
    psum x1, blocking collectives, shards(): total_sq = lax.psum(square_sum, ('az', 'ax'))  37.3 us
    psum x2, blocking collectives, define_the_loads(): local_array = lax.psum(local_array, axis_name=j0)  26.8 us
    slice x2, other arithmetic, with_halo(): last = lax.slice_in_dim(array, length - width, length, axis=dim)  16.5 us
    ppermute x6, starting transfers between devices, with_halo(): after = lax.ppermute(initial, axis, down)  14.6 us
    ppermute x6, waiting for transfers between devices, with_halo(): before = lax.ppermute(last, axis, up)  14.2 us
    ppermute x6, starting transfers between devices, with_halo(): before = lax.ppermute(last, axis, up)  11.1 us
    another operation x4, other arithmetic, second_half(): jnp.stack([back_press, back_az, back_ax, back_rad])  10.7 us
    concatenate x3, other arithmetic, with_halo(): array = jnp.concatenate([before, array, after], axis=dim)  9.38 us
  transfers between devices with their start and end apart: 12, of which 6 were waited for; matrix products, arithmetic and copies ran while one was open for 7% of the time, Pallas kernels for 0%

profile of v1, /device:TPU:0, one launch (start us, length us, event | category | flops | bytes accessed | tf_op | source)
XLA Modules:
  0.0 210.0 jit_solution(2860851315141875054)
XLA Ops:
  0.6 0.9 slice_divide_fusion
  1.5 0.9 slice.363
  2.5 1.0 pad_maximum_fusion.6
  3.7 1.3 collective-permute-start.1
  5.0 3.0 %collective-permute-start = (f32[8,8,2,128]{3,1,2,0:T(8,128)S(1)}, f32[8,8,2,128]{3,1,2,0:T(8,128)S(1)}, u32[]{:S(2)}, u32[]{:S(2)}) collective-permute-start(f32[8,8,2,128]{3,1,2,0:T(8,128)S(1)} %copy.107), channel_id=1, source_target_pairs={{0,1},{1,2},{2,3},{4,5},{5,6},{6,7},{8,9},{9,10},{10,11},{12,13},{... | collective-permute-start | bytes 196616 | tf_op jit(solution)/shard_map/ppermute | solution.py:24
  8.0 2.7 %copy.81 = f32[8,8,16,128]{2,1,3,0:T(8,128)} copy(f32[8,8,16,128]{3,2,1,0:T(8,128)S(1)} %pad_maximum_fusion.6) | data formatting | bytes 1048576 | tf_op jit(solution)/shard_map/concatenate | solution.py:195
  10.7 0.4 fusion.64
  11.1 0.4 fusion.65
  11.6 2.7 %copy.82 = f32[8,8,2,128]{2,1,3,0:T(8,128)} copy(f32[8,8,2,128]{3,1,2,0:T(8,128)S(1)} %collective-permute-done.1) | data formatting | bytes 131072 | tf_op jit(solution)/shard_map/ppermute | solution.py:25
  14.3 2.7 %copy.80 = f32[8,8,2,128]{2,1,3,0:T(8,128)} copy(f32[8,8,2,128]{3,1,2,0:T(8,128)S(1)} %collective-permute-done) | data formatting | bytes 131072 | tf_op jit(solution)/shard_map/ppermute | solution.py:24
  17.0 12.7 %pad_maximum_fusion.5 = (f32[8,2,20,128]{2,1,3,0:T(2,128)S(1)}, f32[8,2,20,128]{2,1,3,0:T(2,128)S(1)}) fusion(f32[8,8,2,128]{2,1,3,0:T(8,128)} %copy.82, f32[8,8,16,128]{2,1,3,0:T(8,128)} %copy.81, f32[8,8,2,128]{2,1,3,0:T(8,128)} %copy.80), kind=kLoop, calls=%fused_computation.47 | loop fusion | flops 163840 | bytes 983040 | tf_op jit(solution)/shard_map/slice | solution.py:22
  30.0 6.1 %collective-permute-start.3 = (f32[8,2,20,128]{3,0,2,1:T(8,128)S(1)}, f32[8,2,20,128]{3,0,2,1:T(8,128)S(1)}, u32[]{:S(2)}, u32[]{:S(2)}) collective-permute-start(f32[8,2,20,128]{3,0,2,1:T(8,128)S(1)} %copy.84), channel_id=1, source_target_pairs={{4,0},{8,4},{12,8},{16,12},{20,16},{24,20},{28,24},{0,28},{5,1},{9... | collective-permute-start | bytes 491528 | tf_op jit(solution)/shard_map/ppermute | solution.py:25
  36.7 0.6 slice.520
  37.3 3.2 %collective-permute-done.3 = f32[8,2,20,128]{3,0,2,1:T(8,128)S(1)} collective-permute-done((f32[8,2,20,128]{3,0,2,1:T(8,128)S(1)}, f32[8,2,20,128]{3,0,2,1:T(8,128)S(1)}, u32[]{:S(2)}, u32[]{:S(2)}) %collective-permute-start.3) | collective-permute-done | bytes 163872 | tf_op jit(solution)/shard_map/ppermute | solution.py:25
  40.6 0.5 copy.86
  41.0 5.3 %collective-permute-done.2 = f32[8,2,20,128]{3,0,2,1:T(8,128)S(1)} collective-permute-done((f32[8,2,20,128]{3,0,2,1:T(8,128)S(1)}, f32[8,2,20,128]{3,0,2,1:T(8,128)S(1)}, u32[]{:S(2)}, u32[]{:S(2)}) %collective-permute-start.2) | collective-permute-done | bytes 163872 | tf_op jit(solution)/shard_map/ppermute | solution.py:24
  46.3 0.5 copy.85
  46.8 7.7 %pad_maximum_fusion = f32[8,12,20,128]{2,1,3,0:T(8,128)S(1)} fusion(f32[8,2,20,128]{2,1,3,0:T(2,128)S(1)} %copy.86, f32[8,8,2,128]{2,1,3,0:T(8,128)} %copy.82, f32[8,8,16,128]{2,1,3,0:T(8,128)} %copy.81, f32[8,8,2,128]{2,1,3,0:T(8,128)} %copy.80, f32[8,2,20,128]{2,1,3,0:T(2,128)S(1)} %copy.85), kind=kLoop, calls=%fused_computation.2 | loop fusion | flops 983040 | bytes 1966080 | tf_op jit(solution)/shard_map/concatenate | solution.py:26
  54.5 0.6 slice_bitcast_fusion.9
  55.0 2.7 %copy-done.2 = f32[8,12,20,128]{2,1,3,0:T(8,128)} copy-done((f32[8,12,20,128]{2,1,3,0:T(8,128)}, f32[8,12,20,128]{2,1,3,0:T(8,128)S(1)}, u32[]{:S(2)}) %copy-start.2) | copy-done | bytes 983064
  58.1 2.5 %fusion.5 = f32[10,18,128]{1,0,2:T(8,128)S(1)} fusion(f32[12,20,128]{1,0,2:T(8,128)S(1)} %get-tuple-element.33, f32[12,20,128]{1,0,2:T(8,128)S(1)} %get-tuple-element.28, f32[12,20,128]{1,0,2:T(8,128)S(1)} %get-tuple-element.29, f32[12,20,128]{1,0,2:T(8,128)S(1)} %get-tuple-element.31, f32[12,20,128]{1,0,2:T(8,128)S(1)} %get-tuple-element.32), kind=kLoop, calls=%fused_computation.20 | loop fusion | flops 253440 | bytes 1013760 | tf_op jit(solution)/shard_map/sub | solution.py:93
  60.6 2.5 %fusion.13 = f32[10,18,128]{1,0,2:T(8,128)S(1)} fusion(f32[12,20,128]{1,0,2:T(8,128)S(1)} %get-tuple-element.33, f32[12,20,128]{1,0,2:T(8,128)S(1)} %get-tuple-element.26, f32[12,20,128]{1,0,2:T(8,128)S(1)} %get-tuple-element.29, f32[12,20,128]{1,0,2:T(8,128)S(1)} %get-tuple-element.31, f32[12,20,128]{1,0,2:T(8,128)S(1)} %get-tuple-element.32), kind=kLoop, calls=%fused_computation.32 | loop fusion | flops 253440 | bytes 1013760 | tf_op jit(solution)/shard_map/sub | solution.py:89
  63.1 2.0 fusion.62
  65.1 0.5 fusion.60
  65.6 0.7 fusion.69
  66.4 3.3 %gather_fusion = f32[512]{0:T(512)S(1)} fusion(f32[128]{0:T(128)S(1)} %reshape_squeeze.3, s32[1024]{0:T(1024)S(1)} %pad_clamp_fusion), kind=kCustom, calls=%fused_computation | custom fusion | bytes 6144 | tf_op jit(solution)/shard_map/gather | solution.py:205
  69.8 0.6 multiply_reduce_fusion
  70.4 37.3 %psum.21 = f32[]{:T(128)} all-reduce(f32[]{:T(128)} %get-tuple-element.11), channel_id=1, replica_groups=mesh['az'=8,'ax'=4] {'az','ax'}, use_global_device_ids=true, to_apply=%region_1.2 | all-reduce | flops 1 | bytes 8 | tf_op jit(solution)/shard_map/psum | solution.py:213
  108.3 4.1 %scatter_custom_fusion = f32[128]{0:T(128)S(1)} fusion(s32[512]{0:T(512)S(1)} %compare_select_fusion, f32[512]{0:T(512)S(1)} %divide_select_fusion, f32[]{:T(128)} %constant.19.clone.1), kind=kCustom, calls=%fused_computation.159 | custom fusion | flops 512 | bytes 516 | tf_op jit(solution)/shard_map/scatter-add | solution.py:218
  112.7 1.3 collective-permute-start.5
  114.0 3.0 %collective-permute-start.4 = (f32[1,8,1,128]{3,1,2,0:T(8,128)S(1)}, f32[1,8,1,128]{3,1,2,0:T(8,128)S(1)}, u32[]{:S(2)}, u32[]{:S(2)}) collective-permute-start(f32[1,8,1,128]{3,1,2,0:T(8,128)S(1)} %get-tuple-element.60), channel_id=1, source_target_pairs={{0,1},{1,2},{2,3},{4,5},{5,6},{6,7},{8,9},{9,10},{10,11},{12,13},{... | collective-permute-start | bytes 12296 | tf_op jit(solution)/shard_map/ppermute | solution.py:24
  117.0 0.8 collective-permute-done.4
  118.0 4.3 %collective-permute-start.7 = (f32[1,1,18,128]{2,1,3,0:T(1,128)S(1)}, f32[1,1,18,128]{2,1,3,0:T(1,128)S(1)}, u32[]{:S(2)}, u32[]{:S(2)}) collective-permute-start(f32[1,1,18,128]{2,1,3,0:T(1,128)S(1)} %copy.89), channel_id=1, source_target_pairs={{4,0},{8,4},{12,8},{16,12},{20,16},{24,20},{28,24},{0,28},{5,1},{9... | collective-permute-start | bytes 27656 | tf_op jit(solution)/shard_map/ppermute | solution.py:25
  123.1 1.0 copy.112
  124.4 4.9 %collective-permute-done.6 = f32[1,1,18,128]{2,1,3,0:T(1,128)S(1)} collective-permute-done((f32[1,1,18,128]{2,1,3,0:T(1,128)S(1)}, f32[1,1,18,128]{2,1,3,0:T(1,128)S(1)}, u32[]{:S(2)}, u32[]{:S(2)}) %collective-permute-start.6) | collective-permute-done | bytes 9248 | tf_op jit(solution)/shard_map/ppermute | solution.py:24
  129.3 4.1 %fusion.21 = (f32[10,18,128]{1,0,2:T(8,128)}, f32[10,18,128]{1,0,2:T(8,128)S(1)}, f32[10,18,128]{1,0,2:T(8,128)}) fusion(f32[8,12,20,128]{2,1,3,0:T(8,128)} %copy-done.2, f32[1,1,18,128]{2,1,3,0:T(1,128)S(1)} %collective-permute-done.7, f32[1,8,18,128]{2,1,3,0:T(8,128)S(1)} %copy.90, f32[1,1,18,128]{2,1,3,0:T(1,128)S(1)} %collective-permute-done.6), kind=kLoop, calls=%fused_computation.54 | loop fusion | flops 138240 | bytes 645120 | tf_op jit(solution)/shard_map/mul | solution.py:74
  133.7 0.5 fusion.48
  134.3 0.5 fusion.77
  135.4 0.5 copy.95
  135.9 1.3 collective-permute-start.9
  137.2 0.5 copy.94
  137.7 3.0 %collective-permute-start.8 = (f32[3,8,1,128]{3,1,2,0:T(8,128)S(1)}, f32[3,8,1,128]{3,1,2,0:T(8,128)S(1)}, u32[]{:S(2)}, u32[]{:S(2)}) collective-permute-start(f32[3,8,1,128]{3,1,2,0:T(8,128)S(1)} %copy.94), channel_id=1, source_target_pairs={{0,1},{1,2},{2,3},{4,5},{5,6},{6,7},{8,9},{9,10},{10,11},{12,13},{... | collective-permute-start | bytes 36872 | tf_op jit(solution)/shard_map/ppermute | solution.py:24
  140.7 2.6 %slice_bitcast_fusion.3 = f32[10,18,128]{1,0,2:T(8,128)} fusion(f32[8,12,20,128]{2,1,3,0:T(8,128)} %copy-done.2), kind=kLoop, calls=%fused_computation.12 | loop fusion | bytes 184320 | tf_op jit(solution)/shard_map/squeeze | solution.py:136
  143.4 0.6 copy.97
  143.9 0.6 copy.96
  144.5 3.8 %pad_maximum_fusion.12 = (f32[3,1,18,128]{2,1,3,0:T(1,128)S(1)}, f32[3,1,18,128]{2,1,3,0:T(1,128)S(1)}) fusion(f32[3,8,1,128]{2,1,3,0:T(8,128)S(1)} %copy.97, f32[3,8,1,128]{2,1,3,0:T(8,128)S(1)} %copy.96, f32[1,8,16,128]{2,1,3,0:T(8,128)} %copy-done.7, f32[1,8,16,128]{2,1,3,0:T(8,128)} %copy-done.5, f32[1,8,16,128]{2,1,3,0:T(8,128)} %copy-done.3), kind=kLoop, calls=%fused_computation.127 | loop fusion | flops 55296 | bytes 276480 | tf_op jit(solution)/shard_map/slice | solution.py:22
  148.4 0.4 collective-permute-start.11
  148.7 1.7 collective-permute-start.10
  150.4 1.2 maximum_bitcast_fusion
  151.7 3.3 %collective-permute-done.11 = f32[3,1,18,128]{2,1,3,0:T(1,128)S(1)} collective-permute-done((f32[3,1,18,128]{2,1,3,0:T(1,128)S(1)}, f32[3,1,18,128]{2,1,3,0:T(1,128)S(1)}, u32[]{:S(2)}, u32[]{:S(2)}) %collective-permute-start.11) | collective-permute-done | bytes 27680 | tf_op jit(solution)/shard_map/ppermute | solution.py:25
  155.0 3.1 %collective-permute-done.10 = f32[3,1,18,128]{2,1,3,0:T(1,128)S(1)} collective-permute-done((f32[3,1,18,128]{2,1,3,0:T(1,128)S(1)}, f32[3,1,18,128]{2,1,3,0:T(1,128)S(1)}, u32[]{:S(2)}, u32[]{:S(2)}) %collective-permute-start.10) | collective-permute-done | bytes 27680 | tf_op jit(solution)/shard_map/ppermute | solution.py:24
  158.1 1.7 pad_maximum_fusion.1
  159.9 4.9 %multiply_multiply_fusion.1 = (f32[10,18,128]{1,0,2:T(8,128)}, f32[10,18,128]{1,0,2:T(8,128)}, f32[10,18,128]{1,0,2:T(8,128)S(1)}, f32[10,18,128]{1,0,2:T(8,128)...) fusion(f32[8,12,20,128]{2,1,3,0:T(8,128)} %copy-done.2, ...), kind=kLoop, calls=%fused_computation.50 | loop fusion | flops 207360 | bytes 1290368 | tf_op jit(solution)/shard_map/mul | solution.py:142
  164.8 1.8 slice_bitcast_fusion
  166.6 1.7 fusion.22
  168.2 0.7 fusion.41
  169.2 3.1 %fusion.33 = f32[1,8,16,128]{2,1,3,0:T(8,128)S(1)} fusion(f32[10,18,128]{1,0,2:T(8,128)} %get-tuple-element.18, f32[10,18,128]{1,0,2:T(8,128)} %get-tuple-element.20, f32[10,18,128]{1,0,2:T(8,128)} %get-tuple-element.37), kind=kLoop, calls=%fused_computation.69 | loop fusion | flops 81920 | bytes 393216 | tf_op jit(solution)/shard_map/stack | solution.py:154
  172.5 1.9 fusion.37
  174.6 5.0 %fusion.40 = f32[1,8,16,128]{2,1,3,0:T(8,128)S(1)} fusion(f32[10,18,128]{1,0,2:T(8,128)} %get-tuple-element.36, f32[10,18,128]{1,0,2:T(8,128)} %get-tuple-element.16, f32[10,18,128]{1,0,2:T(8,128)} %get-tuple-element.15, f32[10,18,128]{1,0,2:T(8,128)} %get-tuple-element.25, f32[10,18,128]{1,0,2:T(8,128)} %get-tuple-element.23, ...), kind=kLoop, calls=%fused_computation.80 | loop fusion | flops 229376 | bytes 852096 | tf_op jit(solution)/shard_map/stack | solution.py:154
  179.8 0.8 slice_multiply_fusion.4
  180.8 7.8 %psum.22 = f32[64]{0:T(128)S(1)} all-reduce(f32[64]{0:T(128)S(1)} %convolution_bitcast_fusion), channel_id=1, replica_groups=mesh['az'=8,'ax'=4] {'ax'}, use_global_device_ids=true, to_apply=%region_3.4 | all-reduce | flops 64 | bytes 512 | tf_op jit(solution)/shard_map/psum | solution.py:13
  188.6 19.0 %psum.23 = f32[64]{0:T(128)S(1)} all-reduce(f32[64]{0:T(128)S(1)} %psum.22), channel_id=1, replica_groups=mesh['az'=8,'ax'=4] {'az'}, use_global_device_ids=true, to_apply=%region_4.5 | all-reduce | flops 64 | bytes 512 | tf_op jit(solution)/shard_map/psum | solution.py:13
  207.6 0.5 broadcast_multiply_fusion
  208.1 0.7 pad_maximum_fusion.7
  (82 shorter events, 5.1 us)
Async XLA Ops:
  0.6 10.1 %copy-start = (f32[64]{0:T(128)S(1)}, f32[64]{0:T(128)}, u32[]{:S(2)}) copy-start(f32[64]{0:T(128)} %param.13) | copy-start | bytes 772
  2.5 8.2 %copy-start.12 = (f32[4,8,16,128]{3,2,1,0:T(8,128)S(1)}, f32[4,8,16,128]{3,2,1,0:T(8,128)}, u32[]{:S(2)}) copy-start(f32[4,8,16,128]{3,2,1,0:T(8,128)} %param.12) | copy-start | bytes 786436
  3.5 7.2 %copy-start.17 = (s32[8,16]{1,0:T(8,128)S(1)}, s32[8,16]{1,0:T(8,128)}, u32[]{:S(2)}) copy-start(s32[8,16]{1,0:T(8,128)} %param.14) | copy-start | bytes 1540
  3.5 7.6 %copy-start.16 = (s32[8,16]{1,0:T(8,128)S(1)}, s32[8,16]{1,0:T(8,128)}, u32[]{:S(2)}) copy-start(s32[8,16]{1,0:T(8,128)} %param.15) | copy-start | bytes 1540
  3.5 7.6 %copy-start.18 = (f32[64]{0:T(128)S(1)}, f32[64]{0:T(128)}, u32[]{:S(2)}) copy-start(f32[64]{0:T(128)} %param.16) | copy-start | bytes 772
  3.6 8.0 %copy-start.13 = (s32[512]{0:T(512)S(1)}, s32[512]{0:T(512)}, u32[]{:S(2)}) copy-start(s32[512]{0:T(512)} %param.18) | copy-start | bytes 6148
  3.6 8.0 %copy-start.14 = (s32[512]{0:T(512)S(1)}, s32[512]{0:T(512)}, u32[]{:S(2)}) copy-start(s32[512]{0:T(512)} %param.17) | copy-start | bytes 6148
  3.7 8.0 %collective-permute-start.1 = (f32[8,8,2,128]{3,1,2,0:T(8,128)S(1)}, f32[8,8,2,128]{3,1,2,0:T(8,128)S(1)}, u32[]{:S(2)}, u32[]{:S(2)}) collective-permute-start(f32[8,8,2,128]{3,1,2,0:T(8,128)S(1)} %copy.108), channel_id=1, source_target_pairs={{1,0},{2,1},{3,2},{5,4},{6,5},{7,6},{9,8},{10,9},{11,10},{13,12},{... | collective-permute-start | bytes 196616 | tf_op jit(solution)/shard_map/ppermute | solution.py:25
  5.0 9.3 %collective-permute-start = (f32[8,8,2,128]{3,1,2,0:T(8,128)S(1)}, f32[8,8,2,128]{3,1,2,0:T(8,128)S(1)}, u32[]{:S(2)}, u32[]{:S(2)}) collective-permute-start(f32[8,8,2,128]{3,1,2,0:T(8,128)S(1)} %copy.107), channel_id=1, source_target_pairs={{0,1},{1,2},{2,3},{4,5},{5,6},{6,7},{8,9},{9,10},{10,11},{12,13},{... | collective-permute-start | bytes 196616 | tf_op jit(solution)/shard_map/ppermute | solution.py:24
  30.0 10.5 %collective-permute-start.3 = (f32[8,2,20,128]{3,0,2,1:T(8,128)S(1)}, f32[8,2,20,128]{3,0,2,1:T(8,128)S(1)}, u32[]{:S(2)}, u32[]{:S(2)}) collective-permute-start(f32[8,2,20,128]{3,0,2,1:T(8,128)S(1)} %copy.84), channel_id=1, source_target_pairs={{4,0},{8,4},{12,8},{16,12},{20,16},{24,20},{28,24},{0,28},{5,1},{9... | collective-permute-start | bytes 491528 | tf_op jit(solution)/shard_map/ppermute | solution.py:25
  36.5 9.9 %collective-permute-start.2 = (f32[8,2,20,128]{3,0,2,1:T(8,128)S(1)}, f32[8,2,20,128]{3,0,2,1:T(8,128)S(1)}, u32[]{:S(2)}, u32[]{:S(2)}) collective-permute-start(f32[8,2,20,128]{3,0,2,1:T(8,128)S(1)} %copy.83), channel_id=1, source_target_pairs={{0,4},{4,8},{8,12},{12,16},{16,20},{20,24},{24,28},{28,0},{1,5},{5... | collective-permute-start | bytes 491528 | tf_op jit(solution)/shard_map/ppermute | solution.py:24
  54.5 3.3 %copy-start.2 = (f32[8,12,20,128]{2,1,3,0:T(8,128)}, f32[8,12,20,128]{2,1,3,0:T(8,128)S(1)}, u32[]{:S(2)}) copy-start(f32[8,12,20,128]{2,1,3,0:T(8,128)S(1)} %pad_maximum_fusion) | copy-start | bytes 2949124
  65.1 4.6 %copy-start.15 = (f32[512]{0:T(512)S(1)}, f32[512]{0:T(512)}, u32[]{:S(2)}) copy-start(f32[512]{0:T(512)} %param.19) | copy-start | bytes 6148
  65.6 57.5 %slice-start = ((f32[4,8,16,128]{3,2,1,0:T(8,128)}), f32[1,8,16,128]{3,2,1,0:T(8,128)S(1)}, s32[]{:S(2)}) async-start(f32[4,8,16,128]{3,2,1,0:T(8,128)} %param.10), calls=%async_computation | async-start | bytes 131072 | tf_op jit(solution)/shard_map/slice | solution.py:209
  112.7 4.3 %collective-permute-start.5 = (f32[1,8,1,128]{3,1,2,0:T(8,128)S(1)}, f32[1,8,1,128]{3,1,2,0:T(8,128)S(1)}, u32[]{:S(2)}, u32[]{:S(2)}) collective-permute-start(f32[1,8,1,128]{3,1,2,0:T(8,128)S(1)} %get-tuple-element.61), channel_id=1, source_target_pairs={{1,0},{2,1},{3,2},{5,4},{6,5},{7,6},{9,8},{10,9},{11,10},{13,12},{... | collective-permute-start | bytes 12296 | tf_op jit(solution)/shard_map/ppermute | solution.py:25
  114.0 3.8 %collective-permute-start.4 = (f32[1,8,1,128]{3,1,2,0:T(8,128)S(1)}, f32[1,8,1,128]{3,1,2,0:T(8,128)S(1)}, u32[]{:S(2)}, u32[]{:S(2)}) collective-permute-start(f32[1,8,1,128]{3,1,2,0:T(8,128)S(1)} %get-tuple-element.60), channel_id=1, source_target_pairs={{0,1},{1,2},{2,3},{4,5},{5,6},{6,7},{8,9},{9,10},{10,11},{12,13},{... | collective-permute-start | bytes 12296 | tf_op jit(solution)/shard_map/ppermute | solution.py:24
  118.0 6.4 %collective-permute-start.7 = (f32[1,1,18,128]{2,1,3,0:T(1,128)S(1)}, f32[1,1,18,128]{2,1,3,0:T(1,128)S(1)}, u32[]{:S(2)}, u32[]{:S(2)}) collective-permute-start(f32[1,1,18,128]{2,1,3,0:T(1,128)S(1)} %copy.89), channel_id=1, source_target_pairs={{4,0},{8,4},{12,8},{16,12},{20,16},{24,20},{28,24},{0,28},{5,1},{9... | collective-permute-start | bytes 27656 | tf_op jit(solution)/shard_map/ppermute | solution.py:25
  122.3 7.0 %collective-permute-start.6 = (f32[1,1,18,128]{2,1,3,0:T(1,128)S(1)}, f32[1,1,18,128]{2,1,3,0:T(1,128)S(1)}, u32[]{:S(2)}, u32[]{:S(2)}) collective-permute-start(f32[1,1,18,128]{2,1,3,0:T(1,128)S(1)} %copy.88), channel_id=1, source_target_pairs={{0,4},{4,8},{8,12},{12,16},{16,20},{20,24},{24,28},{28,0},{1,5},{5... | collective-permute-start | bytes 27656 | tf_op jit(solution)/shard_map/ppermute | solution.py:24
  124.4 9.1 %copy-start.9 = (f32[1,8,18,128]{2,1,3,0:T(8,128)}, f32[1,8,18,128]{2,1,3,0:T(8,128)S(1)}, u32[]{:S(2)}) copy-start(f32[1,8,18,128]{2,1,3,0:T(8,128)S(1)} %copy.90) | copy-start | bytes 221188
  134.2 0.8 copy-start.3
  134.2 1.0 copy-start.5
  134.2 1.1 copy-start.7
  135.9 7.5 %collective-permute-start.9 = (f32[3,8,1,128]{3,1,2,0:T(8,128)S(1)}, f32[3,8,1,128]{3,1,2,0:T(8,128)S(1)}, u32[]{:S(2)}, u32[]{:S(2)}) collective-permute-start(f32[3,8,1,128]{3,1,2,0:T(8,128)S(1)} %copy.95), channel_id=1, source_target_pairs={{1,0},{2,1},{3,2},{5,4},{6,5},{7,6},{9,8},{10,9},{11,10},{13,12},{... | collective-permute-start | bytes 36872 | tf_op jit(solution)/shard_map/ppermute | solution.py:25
  137.7 6.3 %collective-permute-start.8 = (f32[3,8,1,128]{3,1,2,0:T(8,128)S(1)}, f32[3,8,1,128]{3,1,2,0:T(8,128)S(1)}, u32[]{:S(2)}, u32[]{:S(2)}) collective-permute-start(f32[3,8,1,128]{3,1,2,0:T(8,128)S(1)} %copy.94), channel_id=1, source_target_pairs={{0,1},{1,2},{2,3},{4,5},{5,6},{6,7},{8,9},{9,10},{10,11},{12,13},{... | collective-permute-start | bytes 36872 | tf_op jit(solution)/shard_map/ppermute | solution.py:24
  144.5 5.9 %copy-start.10 = (f32[1,8,18,128]{2,1,3,0:T(8,128)S(1)}, f32[1,8,18,128]{2,1,3,0:T(8,128)}, u32[]{:S(2)}) copy-start(f32[1,8,18,128]{2,1,3,0:T(8,128)} %copy-done.9) | copy-start | bytes 221188
  144.5 13.6 %copy-start.4 = (f32[1,8,16,128]{2,1,3,0:T(8,128)S(1)}, f32[1,8,16,128]{2,1,3,0:T(8,128)}, u32[]{:S(2)}) copy-start(f32[1,8,16,128]{2,1,3,0:T(8,128)} %copy-done.3) | copy-start | bytes 196612
  144.5 13.6 %copy-start.6 = (f32[1,8,16,128]{2,1,3,0:T(8,128)S(1)}, f32[1,8,16,128]{2,1,3,0:T(8,128)}, u32[]{:S(2)}) copy-start(f32[1,8,16,128]{2,1,3,0:T(8,128)} %copy-done.5) | copy-start | bytes 196612
  144.5 13.6 %copy-start.8 = (f32[1,8,16,128]{2,1,3,0:T(8,128)S(1)}, f32[1,8,16,128]{2,1,3,0:T(8,128)}, u32[]{:S(2)}) copy-start(f32[1,8,16,128]{2,1,3,0:T(8,128)} %copy-done.7) | copy-start | bytes 196612
  148.4 6.6 %collective-permute-start.11 = (f32[3,1,18,128]{2,1,3,0:T(1,128)S(1)}, f32[3,1,18,128]{2,1,3,0:T(1,128)S(1)}, u32[]{:S(2)}, u32[]{:S(2)}) collective-permute-start(f32[3,1,18,128]{2,1,3,0:T(1,128)S(1)} %get-tuple-element.35), channel_id=1, source_target_pairs={{4,0},{8,4},{12,8},{16,12},{20,16},{24,20},{28,24},{0,28},{5,1},{9... | collective-permute-start | bytes 82952 | tf_op jit(solution)/shard_map/ppermute | solution.py:25
  148.7 9.4 %collective-permute-start.10 = (f32[3,1,18,128]{2,1,3,0:T(1,128)S(1)}, f32[3,1,18,128]{2,1,3,0:T(1,128)S(1)}, u32[]{:S(2)}, u32[]{:S(2)}) collective-permute-start(f32[3,1,18,128]{2,1,3,0:T(1,128)S(1)} %get-tuple-element.34), channel_id=1, source_target_pairs={{0,4},{4,8},{8,12},{12,16},{16,20},{20,24},{24,28},{28,0},{1,5},{5... | collective-permute-start | bytes 82952 | tf_op jit(solution)/shard_map/ppermute | solution.py:24
  166.5 1.7 copy-start.11
  174.6 34.2 %copy-start.1 = (f32[64]{0:T(128)S(1)}, f32[64]{0:T(128)}, u32[]{:S(2)}) copy-start(f32[64]{0:T(128)} %param.13) | copy-start | bytes 772
